TPU v7x, 512 devices: a whole 4x8x8 slice. The times are simulated.
512 devices in a mesh: req: 64 (over z, x, core), tp: 8 (over y).
Axes of the slice: x: 4, y: 8, z: 8, core: 2. Of those that a mesh axis runs over, the one named last changes fastest.
Arguments:
- queries: bfloat16 [16384, 7168], P('req', 'tp'), may hold values from -200 to 200
- key_value: bfloat16 [2, 16384, 1024], P(None, 'req', 'tp'), may hold values from -8 to 8
- segment: int32 [16384], P('req'), may hold values from 0 to 31, never falling along the last dimension, each value on 1 to 1024 neighbouring positions
- residual: bfloat16 [16384, 7168], P('req', 'tp'), may hold values from -4 to 4
- out_weight: bfloat16 [7168, 7168], P('tp', 'req'), may hold values from -0.0625 to 0.0625
- head_gain: bfloat16 [7168], P('tp'), may hold values from 0.099609375 to 1.8984375
- vocab_weight: bfloat16 [7168, 64000], P('tp', 'req'), may hold values from -0.21875 to 0.21875
Outputs:
- hidden: bfloat16 [16384, 7168], P('req', 'tp')
- key_cache: bfloat16 [16384, 1024], P('req', 'tp')
- last_norm: float32 [32], replicated
- top_logit: float32 [32], replicated
Inputs may be any that keep to these rules, and one draw needn't show every extreme that they name: `segment`: ids never fall; each of the 32 requests has 1 to 1024 tokens, one has exactly 1024.
All inputs are finite; a program needn't handle non-finite values.
Results may differ from a plain program's by a relative error of at most 0.013.
Values may be sent and summed in bfloat16 or wider, within the bound.
No kernel may reach another device: no remote copies, remote signals or barrier semaphores. Data moves between devices by JAX's collectives and lax.ppermute only.
A program may use at most 128 MiB of HBM per device.

v0:
```python
import jax
import jax.numpy as jnp
from jax import lax
from jax.sharding import Mesh, PartitionSpec as P

D = 7168
HD = 128
GROUP = 7
REACH = 4
REQ = ("z", "x", "c")
theta = 5000000.0
eps = 1e-05
masked_score = -1e30


def from_behind(value, axis, steps):
    count = lax.axis_size(axis)
    initial, last = (max(0, -steps), min(count, count - steps))
    return lax.ppermute(value, axis, [(source, source + steps) for source in range(initial, last)])


def butterfly(value, axis, combine):
    count = lax.axis_size(axis)
    stride = 1
    while stride < count:
        other = lax.ppermute(value, axis, [(source, source ^ stride) for source in range(count)])
        value = combine(value, other)
        stride *= 2
    return value


def halving_scatter(value, axis):
    count = lax.axis_size(axis)
    index = lax.axis_index(axis)
    rows, width = (value.shape[1], value.shape[2])
    held = jnp.moveaxis(value, 0, 1)
    bit = 1
    while bit < count:
        mine = index // bit % 2
        pairs = held.reshape(rows, held.shape[1] // 2, 2, width)
        keep = lax.dynamic_index_in_dim(pairs, mine, 2, keepdims=False)
        give = lax.dynamic_index_in_dim(pairs, 1 - mine, 2, keepdims=False)
        moved = lax.ppermute(give, axis, [(source, source ^ bit) for source in range(count)])
        held = (keep.astype(jnp.float32) + moved.astype(jnp.float32)).astype(value.dtype)
        bit *= 2
    return held.reshape(rows, width).astype(jnp.float32)


def rope_tables(positions, width):
    half_width = width // 2
    frequency = theta ** (-(jnp.arange(half_width, dtype=jnp.float32) * 2.0 / width))
    angles = positions[:, None] * frequency[None, :]
    return (jnp.cos(angles), jnp.sin(angles))


def rotate(values, cosine, sine_table):
    half_width = values.shape[-1] // 2
    first_half = values[..., :half_width]
    second_half = values[..., half_width:]
    table_shape = (cosine.shape[0],) + (1,) * (values.ndim - 2) + (half_width,)
    cosine = cosine.reshape(table_shape)
    sine_table = sine_table.reshape(table_shape)
    return jnp.concatenate(
        [
            first_half * cosine - second_half * sine_table,
            second_half * cosine + first_half * sine_table,
        ],
        axis=-1,
    )


def local(queries, key_value, segment, residual, out_weight, head_gain, vocab_weight):
    tok_rows = segment.shape[0]
    heads_kv = key_value.shape[2] // HD
    requests = lax.axis_size(REQ) // 2
    devices_req = lax.axis_size(REQ)
    device = lax.axis_index(REQ)
    request_ids = jnp.arange(requests, dtype=jnp.int32)
    own_kv = key_value
    width = own_kv.shape[2]
    seg_rows = -(-tok_rows // width)
    seg_flat = jnp.pad(segment, (0, seg_rows * width - tok_rows)).astype(jnp.bfloat16)
    packed = jnp.concatenate(
        [own_kv.reshape(2 * tok_rows, width), seg_flat.reshape(seg_rows, width)], axis=0
    )
    parts_kv, parts_seg = ([], [])
    for back in range(REACH, 0, -1):
        got = from_behind(packed, REQ, back)
        parts_kv.append(got[: 2 * tok_rows].reshape(own_kv.shape))
        parts_seg.append(got[2 * tok_rows :].reshape(-1)[:tok_rows].astype(jnp.int32))
    parts_kv.append(own_kv)
    parts_seg.append(segment)
    next_first = from_behind(segment[:1], REQ, -1)
    window = jnp.concatenate(parts_kv, axis=1)
    seg_window = jnp.concatenate(parts_seg, axis=0)
    span = window.shape[1]
    key_index_i = (device - REACH) * tok_rows + jnp.arange(span, dtype=jnp.int32)
    valid = key_index_i >= 0
    same = (seg_window[:, None] == seg_window[None, :]) & valid[None, :]
    start_i = jnp.min(jnp.where(same, key_index_i[None, :], jnp.int32(2**30)), axis=1)
    key_index = key_index_i.astype(jnp.float32)
    win_start = start_i.astype(jnp.float32)
    win_pos = key_index - win_start
    own_start = win_start[span - tok_rows :]
    tok_index = key_index[span - tok_rows :]
    positions = win_pos[span - tok_rows :]
    cosine, sine_table = rope_tables(win_pos, HD)
    rot_keys = rotate(
        window[0].astype(jnp.float32).reshape(span, heads_kv, HD), cosine, sine_table
    ).astype(jnp.bfloat16)
    q_cos, q_sin = (cosine[span - tok_rows :], sine_table[span - tok_rows :])
    rot_query = rotate(
        queries.astype(jnp.float32).reshape(tok_rows, heads_kv, GROUP, HD), q_cos, q_sin
    ).astype(jnp.bfloat16)
    key_cache = rot_keys[span - tok_rows :].reshape(tok_rows, heads_kv * HD)
    key_rows = rot_keys
    value_rows = window[1].reshape(span, heads_kv, HD)
    q_seg = segment
    allowed = (
        (seg_window[None, :] == q_seg[:, None])
        & valid[None, :]
        & (key_index[None, :] <= tok_index[:, None])
    )
    scale = HD ** (-0.5)
    scores_part = (
        jnp.einsum("qhgd,khd->hgqk", rot_query, key_rows, preferred_element_type=jnp.float32)
        * scale
    )
    scores = jnp.where(allowed[None, None], scores_part, masked_score)
    peak = jnp.max(scores, axis=3, keepdims=True)
    weights = jnp.exp(scores - peak)
    total = jnp.sum(weights, axis=3)
    context = jnp.einsum(
        "hgqk,khd->qhgd",
        weights.astype(jnp.bfloat16),
        value_rows,
        preferred_element_type=jnp.float32,
    )
    context = context / jnp.transpose(total, (2, 0, 1))[..., None]
    attended = context.astype(jnp.bfloat16).reshape(tok_rows, heads_kv * GROUP * HD)
    following = jnp.concatenate([segment[1:], next_first])
    is_last_dev = device == devices_req - 1
    is_end = following != segment
    is_end = is_end.at[tok_rows - 1].set(is_end[tok_rows - 1] | is_last_dev)
    select = (is_end[:, None] & (segment[:, None] == request_ids[None, :])).astype(jnp.bfloat16)
    end_rows = lax.dot_general(
        select,
        jnp.concatenate([attended, residual], axis=1),
        (((0,), (0,)), ((), ())),
        preferred_element_type=jnp.float32,
    ).astype(jnp.bfloat16)
    end_rows = butterfly(end_rows, REQ, jnp.add)
    attended, end_rows = lax.optimization_barrier((attended, end_rows))
    end_att, end_res = (end_rows[:, : attended.shape[1]], end_rows[:, attended.shape[1] :])
    groups = lax.axis_size("tp")
    chip_half = lax.all_gather(out_weight, ("z", "x"), axis=1, tiled=True)
    halves = lax.all_gather(chip_half, "c", axis=0, tiled=False)
    cores, k_rows = (halves.shape[0], halves.shape[1])
    per_group = halves.shape[2] // (groups * out_weight.shape[1])
    halves = halves.reshape(cores, k_rows, groups, per_group, out_weight.shape[1])
    both = jnp.einsum(
        "tk,ckgin->gticn",
        jnp.concatenate([attended, end_att], axis=0),
        halves,
        preferred_element_type=jnp.float32,
    ).astype(jnp.bfloat16)
    both = both.reshape(groups, both.shape[1], -1)
    end_part = both[:, tok_rows:]
    end_sum = halving_scatter(end_part, "tp")
    both, end_sum = lax.optimization_barrier((both, end_sum))
    own_share = lax.psum_scatter(both, "tp", scatter_dimension=0, tiled=True)[0, :tok_rows]
    own_share = own_share.astype(jnp.float32)
    hidden = (residual.astype(jnp.float32) + own_share).astype(jnp.bfloat16)
    last_state = (end_res.astype(jnp.float32) + end_sum).astype(jnp.bfloat16).astype(jnp.float32)
    scaled = (last_state * head_gain.astype(jnp.float32)).astype(jnp.bfloat16)
    square_part = jnp.sum(last_state * last_state, axis=1)
    logit_part = jnp.dot(scaled, vocab_weight, preferred_element_type=jnp.float32)
    summed = butterfly(
        jnp.concatenate([logit_part, square_part[:, None]], axis=1).astype(jnp.bfloat16),
        "tp",
        jnp.add,
    ).astype(jnp.float32)
    raw_logits, square_sum = (summed[:, :-1], summed[:, -1])
    mean_square = square_sum / D
    last_norm = jnp.sqrt(mean_square)
    local_top = jnp.max(raw_logits * lax.rsqrt(mean_square + eps)[:, None], axis=1)
    top_logit = butterfly(local_top, REQ, jnp.maximum)
    return (hidden, key_cache, last_norm, top_logit)


def solution(mesh):
    req_size = mesh.shape["req"]
    split = Mesh(mesh.devices.reshape(req_size // 8, 4, 2, mesh.shape["tp"]), REQ + ("tp",))
    placed = (
        P(REQ, "tp"),
        P(None, REQ, "tp"),
        P(REQ),
        P(REQ, "tp"),
        P("tp", REQ),
        P("tp"),
        P("tp", REQ),
    )
    return jax.shard_map(
        local,
        mesh=split,
        in_specs=placed,
        out_specs=(P(REQ, "tp"), P(REQ, "tp"), P(), P()),
        check_vma=False,
    )
```

profile of v0, /device:TPU:56, one launch (start us, length us, event | category | flops | bytes accessed | tf_op | source)
XLA Modules:
  0.0 372.8 jit_solution(6426506884844975606)
XLA Ops:
  8.0 102.5 %all-gather.4.cloned.1.call-done = bf16[896,3584]{0,1:T(8,128)(2,1)} async-done(((bf16[896,112]{0,1:T(8,128)(2,1)}), bf16[896,3584]{0,1:T(8,128)(2,1)}) %all-gather.4.cloned.1.call-update) | async-done | bytes 6422544 | tf_op jit(solution)/shard_map/all_gather | solution.py:156
  112.2 4.0 %collective-permute-start = (bf16[514,128]{1,0:T(8,128)(2,1)S(1)}, bf16[514,128]{1,0:T(8,128)(2,1)}, u32[]{:S(2)}, u32[]{:S(2)}) collective-permute-start(bf16[514,128]{1,0:T(8,128)(2,1)S(1)} %pad_maximum_fusion), channel_id=1, source_target_pairs={{0,32},{8,40},{16,48},{24,56},{32,64},{40,72},{48,80},{56,88},{64,... | collective-permute-start | bytes 394760 | tf_op jit(solution)/shard_map/ppermute | solution.py:19
  121.0 4.4 %collective-permute-start.3 = (bf16[514,128]{1,0:T(8,128)(2,1)S(1)}, bf16[514,128]{1,0:T(8,128)(2,1)}, u32[]{:S(2)}, u32[]{:S(2)}) collective-permute-start(bf16[514,128]{1,0:T(8,128)(2,1)S(1)} %pad_maximum_fusion), channel_id=1, source_target_pairs={{0,8},{8,16},{16,24},{24,32},{32,40},{40,48},{48,56},{56,64},{64,7... | collective-permute-start | bytes 394760 | tf_op jit(solution)/shard_map/ppermute | solution.py:19
  164.8 4.5 %collective-permute-done.6 = bf16[32,1792]{1,0:T(8,128)(2,1)S(1)} collective-permute-done((bf16[32,1792]{1,0:T(8,128)(2,1)S(1)}, bf16[32,1792]{1,0:T(8,128)(2,1)S(1)}, u32[]{:S(2)}, u32[]{:S(2)}) %collective-permute-start.6) | collective-permute-done | bytes 114720 | tf_op jit(solution)/shard_map/ppermute | solution.py:26
  172.9 4.6 %collective-permute-done.7 = bf16[32,1792]{1,0:T(8,128)(2,1)S(1)} collective-permute-done((bf16[32,1792]{1,0:T(8,128)(2,1)S(1)}, bf16[32,1792]{1,0:T(8,128)(2,1)S(1)}, u32[]{:S(2)}, u32[]{:S(2)}) %collective-permute-start.7) | collective-permute-done | bytes 114720 | tf_op jit(solution)/shard_map/ppermute | solution.py:26
  177.6 4.6 %collective-permute-start.8 = (bf16[32,1792]{1,0:T(8,128)(2,1)S(1)}, bf16[32,1792]{1,0:T(8,128)(2,1)S(1)}, u32[]{:S(2)}, u32[]{:S(2)}) collective-permute-start(bf16[32,1792]{1,0:T(8,128)(2,1)S(1)} %add.131), channel_id=1, source_target_pairs={{0,64},{8,72},{16,80},{24,88},{32,96},{40,104},{48,112},{56,120},{... | collective-permute-start | bytes 344072 | tf_op jit(solution)/shard_map/ppermute | solution.py:26
  184.9 5.0 %collective-permute-start.9 = (bf16[32,1792]{1,0:T(8,128)(2,1)S(1)}, bf16[32,1792]{1,0:T(8,128)(2,1)S(1)}, u32[]{:S(2)}, u32[]{:S(2)}) collective-permute-start(bf16[32,1792]{1,0:T(8,128)(2,1)S(1)} %add.132), channel_id=1, source_target_pairs={{0,128},{8,136},{16,144},{24,152},{32,160},{40,168},{48,176},{56,1... | collective-permute-start | bytes 344072 | tf_op jit(solution)/shard_map/ppermute | solution.py:26
  192.8 7.6 %collective-permute-start.10 = (bf16[32,1792]{1,0:T(8,128)(2,1)S(1)}, bf16[32,1792]{1,0:T(8,128)(2,1)S(1)}, u32[]{:S(2)}, u32[]{:S(2)}) collective-permute-start(bf16[32,1792]{1,0:T(8,128)(2,1)S(1)} %add.133), channel_id=1, source_target_pairs={{0,256},{8,264},{16,272},{24,280},{32,288},{40,296},{48,304},{56,3... | collective-permute-start | bytes 344072 | tf_op jit(solution)/shard_map/ppermute | solution.py:26
  205.0 24.7 %reshape.392 = bf16[2,896,8,4,112]{1,0,4,3,2:T(2,128)(2,1)} reshape(bf16[1792,3584]{0,1:T(8,128)(2,1)} %all-gather.6.cloned.1.call-done) | data formatting | bytes 25690112 | tf_op jit(solution)/shard_map/reshape | solution.py:160
  229.7 11.9 %convert_bitcast_fusion = bf16[8,288,4,2,112]{4,1,2,0,3:T(8,128)(2,1)} fusion(bf16[2,896,8,4,112]{1,0,4,3,2:T(2,128)(2,1)} %reshape.392, bf16[32,896]{1,0:T(8,128)(2,1)S(1)} %slice.111, bf16[256,896]{1,0:T(8,128)(2,1)S(1)} %copy-done.2), kind=kOutput, calls=%fused_computation.8 | convolution fusion | flops 3702472704 | bytes 17489920 | tf_op jit(solution)/shard_map/tk,ckgin->gticn/dot_general | solution.py:161
  241.6 9.4 %copy.36 = bf16[8,288,4,2,112]{4,3,2,1,0:T(2,128)(2,1)} copy(bf16[8,288,4,2,112]{4,1,2,0,3:T(8,128)(2,1)} %convert_bitcast_fusion) | data formatting | bytes 8257536 | tf_op jit(solution)/shard_map/convert_element_type | solution.py:166
  251.0 15.5 %reshape.393 = bf16[8,288,896]{2,1,0:T(8,128)(2,1)} reshape(bf16[8,288,4,2,112]{4,3,2,1,0:T(2,128)(2,1)} %copy.36) | data formatting | bytes 8257536 | tf_op jit(solution)/shard_map/reshape | solution.py:167
  270.9 4.5 %collective-permute-done.11 = bf16[32,4,896]{2,0,1:T(8,128)(2,1)S(1)} collective-permute-done((bf16[32,4,896]{2,0,1:T(8,128)(2,1)S(1)}, bf16[32,4,896]{2,0,1:T(8,128)(2,1)S(1)}, u32[]{:S(2)}, u32[]{:S(2)}) %collective-permute-start.11) | collective-permute-done | bytes 229408 | tf_op jit(solution)/shard_map/ppermute | solution.py:43
  275.6 5.0 %collective-permute-start.12 = (bf16[32,2,896]{2,0,1:T(8,128)(2,1)S(1)}, bf16[32,2,896]{2,0,1:T(8,128)(2,1)S(1)}, u32[]{:S(2)}, u32[]{:S(2)}) collective-permute-start(bf16[32,2,896]{2,0,1:T(8,128)(2,1)S(1)} %dynamic-slice_bitcast_fusion.1), channel_id=1, source_target_pairs={{0,2},{1,3},{2,0},{3,1},{4,6},{5,7},{6,4},{7,5},{8,10},{9,11},{10,... | collective-permute-start | bytes 344072 | tf_op jit(solution)/shard_map/ppermute | solution.py:43
  280.6 4.6 %collective-permute-done.12 = bf16[32,2,896]{2,0,1:T(8,128)(2,1)S(1)} collective-permute-done((bf16[32,2,896]{2,0,1:T(8,128)(2,1)S(1)}, bf16[32,2,896]{2,0,1:T(8,128)(2,1)S(1)}, u32[]{:S(2)}, u32[]{:S(2)}) %collective-permute-start.12) | collective-permute-done | bytes 114720 | tf_op jit(solution)/shard_map/ppermute | solution.py:43
  285.2 4.3 %collective-permute-start.13 = (bf16[32,1,896]{2,0,1:T(8,128)(2,1)S(1)}, bf16[32,1,896]{2,0,1:T(8,128)(2,1)S(1)}, u32[]{:S(2)}, u32[]{:S(2)}) collective-permute-start(bf16[32,1,896]{2,0,1:T(8,128)(2,1)S(1)} %constant_dynamic-slice_fusion), channel_id=1, source_target_pairs={{0,4},{1,5},{2,6},{3,7},{4,0},{5,1},{6,2},{7,3},{8,12},{9,13},{10,... | collective-permute-start | bytes 172040 | tf_op jit(solution)/shard_map/ppermute | solution.py:43
  289.5 6.0 %collective-permute-done.13 = bf16[32,1,896]{2,0,1:T(8,128)(2,1)S(1)} collective-permute-done((bf16[32,1,896]{2,0,1:T(8,128)(2,1)S(1)}, bf16[32,1,896]{2,0,1:T(8,128)(2,1)S(1)}, u32[]{:S(2)}, u32[]{:S(2)}) %collective-permute-start.13) | collective-permute-done | bytes 57376 | tf_op jit(solution)/shard_map/ppermute | solution.py:43
  298.5 4.2 %collective-permute-done.14 = bf16[32,1001]{1,0:T(8,128)(2,1)S(1)} collective-permute-done((bf16[32,1001]{1,0:T(8,128)(2,1)S(1)}, bf16[32,1001]{1,0:T(8,128)(2,1)S(1)}, u32[]{:S(2)}, u32[]{:S(2)}) %collective-permute-start.14) | collective-permute-done | bytes 64096 | tf_op jit(solution)/shard_map/ppermute | solution.py:26
  306.0 4.5 %collective-permute-done.15 = bf16[32,1001]{1,0:T(8,128)(2,1)S(1)} collective-permute-done((bf16[32,1001]{1,0:T(8,128)(2,1)S(1)}, bf16[32,1001]{1,0:T(8,128)(2,1)S(1)}, u32[]{:S(2)}, u32[]{:S(2)}) %collective-permute-start.15) | collective-permute-done | bytes 64096 | tf_op jit(solution)/shard_map/ppermute | solution.py:26
  310.5 6.0 %collective-permute-start.16 = (bf16[32,1001]{1,0:T(8,128)(2,1)S(1)}, bf16[32,1001]{1,0:T(8,128)(2,1)S(1)}, u32[]{:S(2)}, u32[]{:S(2)}) collective-permute-start(bf16[32,1001]{1,0:T(8,128)(2,1)S(1)} %add.150), channel_id=1, source_target_pairs={{0,4},{1,5},{2,6},{3,7},{4,0},{5,1},{6,2},{7,3},{8,12},{9,13},{10,... | collective-permute-start | bytes 192200 | tf_op jit(solution)/shard_map/ppermute | solution.py:26
  316.5 5.8 %collective-permute-done.16 = bf16[32,1001]{1,0:T(8,128)(2,1)S(1)} collective-permute-done((bf16[32,1001]{1,0:T(8,128)(2,1)S(1)}, bf16[32,1001]{1,0:T(8,128)(2,1)S(1)}, u32[]{:S(2)}, u32[]{:S(2)}) %collective-permute-start.16) | collective-permute-done | bytes 64096 | tf_op jit(solution)/shard_map/ppermute | solution.py:26
  331.6 5.1 %collective-permute-start.19 = (f32[32]{0:T(128)S(1)}, f32[32]{0:T(128)S(1)}, u32[]{:S(2)}, u32[]{:S(2)}) collective-permute-start(f32[32]{0:T(128)S(1)} %max.19), channel_id=1, source_target_pairs={{0,32},{8,40},{16,48},{24,56},{32,0},{40,8},{48,16},{56,24},{64,96... | collective-permute-start | bytes 392 | tf_op jit(solution)/shard_map/ppermute | solution.py:26
  344.0 8.8 %collective-permute-start.21 = (f32[32]{0:T(128)S(1)}, f32[32]{0:T(128)S(1)}, u32[]{:S(2)}, u32[]{:S(2)}) collective-permute-start(f32[32]{0:T(128)S(1)} %max.21), channel_id=1, source_target_pairs={{0,128},{8,136},{16,144},{24,152},{32,160},{40,168},{48,176},{56,1... | collective-permute-start | bytes 392 | tf_op jit(solution)/shard_map/ppermute | solution.py:26
  358.5 5.2 %collective-permute-done.22 = f32[32]{0:T(128)S(1)} collective-permute-done((f32[32]{0:T(128)S(1)}, f32[32]{0:T(128)S(1)}, u32[]{:S(2)}, u32[]{:S(2)}) %collective-permute-start.22) | collective-permute-done | bytes 160 | tf_op jit(solution)/shard_map/ppermute | solution.py:26
  (121 shorter events, 95.0 us)
Async XLA Ops:
  7.2 103.3 %all-gather.4.cloned.1.call-start = ((), (), s32[]{:S(2)}) async-start(), calls=%async_computation.1 | async-start | bytes 6623232 | tf_op jit(solution)/shard_map/all_gather | solution.py:156
  7.9 197.0 %all-gather.6.cloned.1.call-start = ((), (), s32[]{:S(2)}) async-start(), calls=%async_computation.3 | async-start | bytes 19267584 | tf_op jit(solution)/shard_map/all_gather | solution.py:157
  110.6 253.6 %reduce-scatter.2.cloned.1.call-start = ((), (), s32[]{:S(2)}) async-start(), calls=%async_computation.2 | async-start | bytes 4644864 | tf_op jit(solution)/shard_map/reduce_scatter | solution.py:171
  112.2 23.4 %collective-permute-start = (bf16[514,128]{1,0:T(8,128)(2,1)S(1)}, bf16[514,128]{1,0:T(8,128)(2,1)}, u32[]{:S(2)}, u32[]{:S(2)}) collective-permute-start(bf16[514,128]{1,0:T(8,128)(2,1)S(1)} %pad_maximum_fusion), channel_id=1, source_target_pairs={{0,32},{8,40},{16,48},{24,56},{32,64},{40,72},{48,80},{56,88},{64,... | collective-permute-start | bytes 394760 | tf_op jit(solution)/shard_map/ppermute | solution.py:19
  116.2 20.3 %collective-permute-start.1 = (bf16[514,128]{1,0:T(8,128)(2,1)S(1)}, bf16[514,128]{1,0:T(8,128)(2,1)}, u32[]{:S(2)}, u32[]{:S(2)}) collective-permute-start(bf16[514,128]{1,0:T(8,128)(2,1)S(1)} %pad_maximum_fusion), channel_id=1, source_target_pairs={{0,24},{8,32},{16,40},{24,48},{32,56},{40,64},{48,72},{56,80},{64,... | collective-permute-start | bytes 394760 | tf_op jit(solution)/shard_map/ppermute | solution.py:19
  118.1 19.3 %collective-permute-start.2 = (bf16[514,128]{1,0:T(8,128)(2,1)S(1)}, bf16[514,128]{1,0:T(8,128)(2,1)}, u32[]{:S(2)}, u32[]{:S(2)}) collective-permute-start(bf16[514,128]{1,0:T(8,128)(2,1)S(1)} %pad_maximum_fusion), channel_id=1, source_target_pairs={{0,16},{8,24},{16,32},{24,40},{32,48},{40,56},{48,64},{56,72},{64,... | collective-permute-start | bytes 394760 | tf_op jit(solution)/shard_map/ppermute | solution.py:19
  121.0 17.4 %collective-permute-start.3 = (bf16[514,128]{1,0:T(8,128)(2,1)S(1)}, bf16[514,128]{1,0:T(8,128)(2,1)}, u32[]{:S(2)}, u32[]{:S(2)}) collective-permute-start(bf16[514,128]{1,0:T(8,128)(2,1)S(1)} %pad_maximum_fusion), channel_id=1, source_target_pairs={{0,8},{8,16},{16,24},{24,32},{32,40},{40,48},{48,56},{56,64},{64,7... | collective-permute-start | bytes 394760 | tf_op jit(solution)/shard_map/ppermute | solution.py:19
  126.6 6.9 %collective-permute-start.4 = (s32[1]{0:T(128)}, s32[1]{0:T(128)}, u32[]{:S(2)}, u32[]{:S(2)}) collective-permute-start(s32[1]{0:T(128)} %slice.109), channel_id=1, source_target_pairs={{8,0},{16,8},{24,16},{32,24},{40,32},{48,40},{56,48},{64,56},{72,6... | collective-permute-start | bytes 20 | tf_op jit(solution)/shard_map/ppermute | solution.py:19
  162.0 7.3 %collective-permute-start.6 = (bf16[32,1792]{1,0:T(8,128)(2,1)S(1)}, bf16[32,1792]{1,0:T(8,128)(2,1)S(1)}, u32[]{:S(2)}, u32[]{:S(2)}) collective-permute-start(bf16[32,1792]{1,0:T(8,128)(2,1)S(1)} %add.129), channel_id=1, source_target_pairs={{0,16},{8,24},{16,0},{24,8},{32,48},{40,56},{48,32},{56,40},{64,80... | collective-permute-start | bytes 344072 | tf_op jit(solution)/shard_map/ppermute | solution.py:26
  169.4 8.2 %collective-permute-start.7 = (bf16[32,1792]{1,0:T(8,128)(2,1)S(1)}, bf16[32,1792]{1,0:T(8,128)(2,1)S(1)}, u32[]{:S(2)}, u32[]{:S(2)}) collective-permute-start(bf16[32,1792]{1,0:T(8,128)(2,1)S(1)} %add.130), channel_id=1, source_target_pairs={{0,32},{8,40},{16,48},{24,56},{32,0},{40,8},{48,16},{56,24},{64,96... | collective-permute-start | bytes 344072 | tf_op jit(solution)/shard_map/ppermute | solution.py:26
  177.6 7.3 %collective-permute-start.8 = (bf16[32,1792]{1,0:T(8,128)(2,1)S(1)}, bf16[32,1792]{1,0:T(8,128)(2,1)S(1)}, u32[]{:S(2)}, u32[]{:S(2)}) collective-permute-start(bf16[32,1792]{1,0:T(8,128)(2,1)S(1)} %add.131), channel_id=1, source_target_pairs={{0,64},{8,72},{16,80},{24,88},{32,96},{40,104},{48,112},{56,120},{... | collective-permute-start | bytes 344072 | tf_op jit(solution)/shard_map/ppermute | solution.py:26
  184.9 7.8 %collective-permute-start.9 = (bf16[32,1792]{1,0:T(8,128)(2,1)S(1)}, bf16[32,1792]{1,0:T(8,128)(2,1)S(1)}, u32[]{:S(2)}, u32[]{:S(2)}) collective-permute-start(bf16[32,1792]{1,0:T(8,128)(2,1)S(1)} %add.132), channel_id=1, source_target_pairs={{0,128},{8,136},{16,144},{24,152},{32,160},{40,168},{48,176},{56,1... | collective-permute-start | bytes 344072 | tf_op jit(solution)/shard_map/ppermute | solution.py:26
  192.8 11.2 %collective-permute-start.10 = (bf16[32,1792]{1,0:T(8,128)(2,1)S(1)}, bf16[32,1792]{1,0:T(8,128)(2,1)S(1)}, u32[]{:S(2)}, u32[]{:S(2)}) collective-permute-start(bf16[32,1792]{1,0:T(8,128)(2,1)S(1)} %add.133), channel_id=1, source_target_pairs={{0,256},{8,264},{16,272},{24,280},{32,288},{40,296},{48,304},{56,3... | collective-permute-start | bytes 344072 | tf_op jit(solution)/shard_map/ppermute | solution.py:26
  267.5 7.9 %collective-permute-start.11 = (bf16[32,4,896]{2,0,1:T(8,128)(2,1)S(1)}, bf16[32,4,896]{2,0,1:T(8,128)(2,1)S(1)}, u32[]{:S(2)}, u32[]{:S(2)}) collective-permute-start(bf16[32,4,896]{2,0,1:T(8,128)(2,1)S(1)} %dynamic-slice_bitcast_fusion), channel_id=1, source_target_pairs={{0,1},{1,0},{2,3},{3,2},{4,5},{5,4},{6,7},{7,6},{8,9},{9,8},{10,11... | collective-permute-start | bytes 688136 | tf_op jit(solution)/shard_map/ppermute | solution.py:43
  275.6 9.6 %collective-permute-start.12 = (bf16[32,2,896]{2,0,1:T(8,128)(2,1)S(1)}, bf16[32,2,896]{2,0,1:T(8,128)(2,1)S(1)}, u32[]{:S(2)}, u32[]{:S(2)}) collective-permute-start(bf16[32,2,896]{2,0,1:T(8,128)(2,1)S(1)} %dynamic-slice_bitcast_fusion.1), channel_id=1, source_target_pairs={{0,2},{1,3},{2,0},{3,1},{4,6},{5,7},{6,4},{7,5},{8,10},{9,11},{10,... | collective-permute-start | bytes 344072 | tf_op jit(solution)/shard_map/ppermute | solution.py:43
  285.2 10.4 %collective-permute-start.13 = (bf16[32,1,896]{2,0,1:T(8,128)(2,1)S(1)}, bf16[32,1,896]{2,0,1:T(8,128)(2,1)S(1)}, u32[]{:S(2)}, u32[]{:S(2)}) collective-permute-start(bf16[32,1,896]{2,0,1:T(8,128)(2,1)S(1)} %constant_dynamic-slice_fusion), channel_id=1, source_target_pairs={{0,4},{1,5},{2,6},{3,7},{4,0},{5,1},{6,2},{7,3},{8,12},{9,13},{10,... | collective-permute-start | bytes 172040 | tf_op jit(solution)/shard_map/ppermute | solution.py:43
  296.6 6.2 %collective-permute-start.14 = (bf16[32,1001]{1,0:T(8,128)(2,1)S(1)}, bf16[32,1001]{1,0:T(8,128)(2,1)S(1)}, u32[]{:S(2)}, u32[]{:S(2)}) collective-permute-start(bf16[32,1001]{1,0:T(8,128)(2,1)S(1)} %pad_maximum_fusion.2), channel_id=1, source_target_pairs={{0,1},{1,0},{2,3},{3,2},{4,5},{5,4},{6,7},{7,6},{8,9},{9,8},{10,11... | collective-permute-start | bytes 192200 | tf_op jit(solution)/shard_map/ppermute | solution.py:26
  302.8 7.6 %collective-permute-start.15 = (bf16[32,1001]{1,0:T(8,128)(2,1)S(1)}, bf16[32,1001]{1,0:T(8,128)(2,1)S(1)}, u32[]{:S(2)}, u32[]{:S(2)}) collective-permute-start(bf16[32,1001]{1,0:T(8,128)(2,1)S(1)} %fusion.66), channel_id=1, source_target_pairs={{0,2},{1,3},{2,0},{3,1},{4,6},{5,7},{6,4},{7,5},{8,10},{9,11},{10,... | collective-permute-start | bytes 192200 | tf_op jit(solution)/shard_map/ppermute | solution.py:26
  310.5 11.8 %collective-permute-start.16 = (bf16[32,1001]{1,0:T(8,128)(2,1)S(1)}, bf16[32,1001]{1,0:T(8,128)(2,1)S(1)}, u32[]{:S(2)}, u32[]{:S(2)}) collective-permute-start(bf16[32,1001]{1,0:T(8,128)(2,1)S(1)} %add.150), channel_id=1, source_target_pairs={{0,4},{1,5},{2,6},{3,7},{4,0},{5,1},{6,2},{7,3},{8,12},{9,13},{10,... | collective-permute-start | bytes 192200 | tf_op jit(solution)/shard_map/ppermute | solution.py:26
  326.2 5.4 %collective-permute-start.18 = (f32[32]{0:T(128)S(1)}, f32[32]{0:T(128)S(1)}, u32[]{:S(2)}, u32[]{:S(2)}) collective-permute-start(f32[32]{0:T(128)S(1)} %max.18), channel_id=1, source_target_pairs={{0,16},{8,24},{16,0},{24,8},{32,48},{40,56},{48,32},{56,40},{64,80... | collective-permute-start | bytes 392 | tf_op jit(solution)/shard_map/ppermute | solution.py:26
  331.6 6.9 %collective-permute-start.19 = (f32[32]{0:T(128)S(1)}, f32[32]{0:T(128)S(1)}, u32[]{:S(2)}, u32[]{:S(2)}) collective-permute-start(f32[32]{0:T(128)S(1)} %max.19), channel_id=1, source_target_pairs={{0,32},{8,40},{16,48},{24,56},{32,0},{40,8},{48,16},{56,24},{64,96... | collective-permute-start | bytes 392 | tf_op jit(solution)/shard_map/ppermute | solution.py:26
  338.6 5.4 %collective-permute-start.20 = (f32[32]{0:T(128)S(1)}, f32[32]{0:T(128)S(1)}, u32[]{:S(2)}, u32[]{:S(2)}) collective-permute-start(f32[32]{0:T(128)S(1)} %max.20), channel_id=1, source_target_pairs={{0,64},{8,72},{16,80},{24,88},{32,96},{40,104},{48,112},{56,120},{... | collective-permute-start | bytes 392 | tf_op jit(solution)/shard_map/ppermute | solution.py:26
  344.0 10.3 %collective-permute-start.21 = (f32[32]{0:T(128)S(1)}, f32[32]{0:T(128)S(1)}, u32[]{:S(2)}, u32[]{:S(2)}) collective-permute-start(f32[32]{0:T(128)S(1)} %max.21), channel_id=1, source_target_pairs={{0,128},{8,136},{16,144},{24,152},{32,160},{40,168},{48,176},{56,1... | collective-permute-start | bytes 392 | tf_op jit(solution)/shard_map/ppermute | solution.py:26
  354.3 9.3 %collective-permute-start.22 = (f32[32]{0:T(128)S(1)}, f32[32]{0:T(128)S(1)}, u32[]{:S(2)}, u32[]{:S(2)}) collective-permute-start(f32[32]{0:T(128)S(1)} %max.22), channel_id=1, source_target_pairs={{0,256},{8,264},{16,272},{24,280},{32,288},{40,296},{48,304},{56,3... | collective-permute-start | bytes 392 | tf_op jit(solution)/shard_map/ppermute | solution.py:26
  (7 other events, 626.1 us)
Sparse Core Ops, SparseCore 0:
  11.2 99.2 all-gather.3
  112.6 29.8 all-gather.5
  295.7 56.9 reduce-scatter.1
where the time goes:
time: 375 us; the launch traced here: 373 us
  waiting for transfers between devices  166 us (44%)
  starting transfers between devices  90.3 us (24%)
  local copies, waits for them, and re-layouts  63.7 us (17%)
  other arithmetic  19.2 us (5%)
  matrix products  18.3 us (5%)
  between operations  15 us (4%)
    all_gather x1, waiting for transfers between devices, local(): chip_half = lax.all_gather(out_weight, ('z', 'x'), axis=1, tiled=True)  103 us
    ppermute x15, starting transfers between devices, butterfly(): lax.ppermute(value, axis, [(source, source ^ stride) for source in range(...  63.1 us
    ppermute x15, waiting for transfers between devices, butterfly(): lax.ppermute(value, axis, [(source, source ^ stride) for source in range(...  47.8 us
    reshape x1, local copies, waits for them, and re-layouts, local(): halves.reshape(cores, k_rows, groups, per_group, out_weight.shape[1])  24.7 us
    reshape x1, local copies, waits for them, and re-layouts, local(): both = both.reshape(groups, both.shape[1], -1)  15.5 us
    ppermute x3, waiting for transfers between devices, halving_scatter(): lax.ppermute(give, axis, [(source, source ^ bit) for source in range(coun...  15.1 us
    ppermute x5, starting transfers between devices, from_behind(): lax.ppermute(value, axis, [(source, source + steps) for source in range(i...  14.4 us
    ppermute x3, starting transfers between devices, halving_scatter(): lax.ppermute(give, axis, [(source, source ^ bit) for source in range(coun...  12.7 us
  transfers between devices with their start and end apart: 26, of which 19 were waited for; matrix products, arithmetic and copies ran while one was open for 10% of the time, Pallas kernels for 0%

commit v1 on v0

--- a/solution.py
+++ b/solution.py
@@ -153,7 +153,10 @@
     attended, end_rows = lax.optimization_barrier((attended, end_rows))
     end_att, end_res = (end_rows[:, : attended.shape[1]], end_rows[:, attended.shape[1] :])
     groups = lax.axis_size("tp")
-    chip_half = lax.all_gather(out_weight, ("z", "x"), axis=1, tiled=True)
+    chip_half = jnp.concatenate(
+        lax.all_to_all(jnp.stack([out_weight] * lax.axis_size(("z", "x"))), ("z", "x"), 0, 0),
+        axis=1,
+    )
     halves = lax.all_gather(chip_half, "c", axis=0, tiled=False)
     cores, k_rows = (halves.shape[0], halves.shape[1])
     per_group = halves.shape[2] // (groups * out_weight.shape[1])

time: 375 us -> 426 us (1.14)
  blocking collectives: 0 us -> 158 us
  waiting for transfers between devices: 166 us -> 60 us
    all_to_all x0 -> x1, blocking collectives: none -> 158 us  [local(): lax.all_to_all(jnp.stack([out_weight] * lax.axis_size(('z', 'x'))), ('z',...]
    all_gather x1 -> x0, waiting for transfers between devices: 103 us -> none  [local(): chip_half = lax.all_gather(out_weight, ('z', 'x'), axis=1, tiled=True)]
    reshape x1 -> x0, local copies, waits for them, and re-layouts: 24.7 us -> none  [local(): halves.reshape(cores, k_rows, groups, per_group, out_weight.shape[1])]
    all_gather x0 -> x1, local copies, waits for them, and re-layouts: none -> 18 us  [local(): halves = lax.all_gather(chip_half, 'c', axis=0, tiled=False)]
    another operation x0 -> x2, local copies, waits for them, and re-layouts: none -> 11.1 us  [the longest x1 9.58 us: local(): halves = lax.all_gather(chip_half, 'c', axis=0, tiled=False)]
    ppermute x15, waiting for transfers between devices: 47.8 us -> 43.5 us  [butterfly(): lax.ppermute(value, axis, [(source, source ^ stride) for source in range(...]
  transfers between devices with their start and end apart: 26 -> 25, of which waited for: 19 -> 18; matrix products, arithmetic and copies ran while one was open for 10% -> 8% of each run, Pallas kernels for 0% -> 0%
where the time goes in v1:
time: 426 us; the launch traced here: 423 us
  blocking collectives  158 us (37%)
  starting transfers between devices  89.7 us (21%)
  local copies, waits for them, and re-layouts  65.8 us (15%)
  waiting for transfers between devices  60 us (14%)
  other arithmetic  17.6 us (4%)
  matrix products  16.1 us (4%)
  between operations  15.3 us (4%)
    all_to_all x1, blocking collectives, local(): lax.all_to_all(jnp.stack([out_weight] * lax.axis_size(('z', 'x'))), ('z',...  158 us
    ppermute x15, starting transfers between devices, butterfly(): lax.ppermute(value, axis, [(source, source ^ stride) for source in range(...  63.4 us
    ppermute x15, waiting for transfers between devices, butterfly(): lax.ppermute(value, axis, [(source, source ^ stride) for source in range(...  43.5 us
    all_gather x1, local copies, waits for them, and re-layouts, local(): halves = lax.all_gather(chip_half, 'c', axis=0, tiled=False)  18 us
    ppermute x3, waiting for transfers between devices, halving_scatter(): lax.ppermute(give, axis, [(source, source ^ bit) for source in range(coun...  16.5 us
    reshape x1, local copies, waits for them, and re-layouts, local(): both = both.reshape(groups, both.shape[1], -1)  15.5 us
    ppermute x5, starting transfers between devices, from_behind(): lax.ppermute(value, axis, [(source, source + steps) for source in range(i...  14.5 us
    ppermute x3, starting transfers between devices, halving_scatter(): lax.ppermute(give, axis, [(source, source ^ bit) for source in range(coun...  11.6 us
  transfers between devices with their start and end apart: 25, of which 18 were waited for; matrix products, arithmetic and copies ran while one was open for 8% of the time, Pallas kernels for 0%

profile of v1, /device:TPU:56, one launch (start us, length us, event | category | flops | bytes accessed | tf_op | source)
XLA Modules:
  0.0 422.8 jit_solution(12075701992331295963)
XLA Ops:
  8.8 158.4 %all_to_all.5 = bf16[32,896,112]{1,2,0:T(8,128)(2,1)} all-to-all(bf16[32,896,112]{1,2,0:T(8,128)(2,1)S(1)} %stack.2), channel_id=1, replica_groups=mesh['z'=8,'x'=4,'c'=2,'tp'=8] {'z','x'}, dimensions={0} | all-to-all | bytes 12845056 | tf_op jit(solution)/shard_map/all_to_all | solution.py:157
  167.1 9.6 %copy.60 = bf16[1,896,3584]{2,1,0:T(8,128)(2,1)} copy(bf16[1,896,3584]{1,2,0:T(8,128)(2,1)} %bitcast.140) | data formatting | bytes 12845056 | tf_op jit(solution)/shard_map/all_gather;reshape | solution.py:160
  186.0 4.1 collective-permute-start.3
  227.2 4.5 %collective-permute-done.6 = bf16[32,1792]{1,0:T(8,128)(2,1)S(1)} collective-permute-done((bf16[32,1792]{1,0:T(8,128)(2,1)S(1)}, bf16[32,1792]{1,0:T(8,128)(2,1)S(1)}, u32[]{:S(2)}, u32[]{:S(2)}) %collective-permute-start.6) | collective-permute-done | bytes 114720 | tf_op jit(solution)/shard_map/ppermute | solution.py:26
  231.8 4.2 collective-permute-start.7
  235.9 4.0 collective-permute-done.7
  240.0 4.2 %collective-permute-start.8 = (bf16[32,1792]{1,0:T(8,128)(2,1)S(1)}, bf16[32,1792]{1,0:T(8,128)(2,1)S(1)}, u32[]{:S(2)}, u32[]{:S(2)}) collective-permute-start(bf16[32,1792]{1,0:T(8,128)(2,1)S(1)} %add.131), channel_id=1, source_target_pairs={{0,64},{8,72},{16,80},{24,88},{32,96},{40,104},{48,112},{56,120},{... | collective-permute-start | bytes 344072 | tf_op jit(solution)/shard_map/ppermute | solution.py:26
  254.6 7.0 %collective-permute-start.10 = (bf16[32,1792]{1,0:T(8,128)(2,1)S(1)}, bf16[32,1792]{1,0:T(8,128)(2,1)S(1)}, u32[]{:S(2)}, u32[]{:S(2)}) collective-permute-start(bf16[32,1792]{1,0:T(8,128)(2,1)S(1)} %add.133), channel_id=1, source_target_pairs={{0,256},{8,264},{16,272},{24,280},{32,288},{40,296},{48,304},{56,3... | collective-permute-start | bytes 344072 | tf_op jit(solution)/shard_map/ppermute | solution.py:26
  266.4 18.0 %copy.61 = bf16[2,896,3584]{1,2,0:T(8,128)(2,1)} copy(bf16[2,896,3584]{2,1,0:T(8,128)(2,1)} %all-gather.2.cloned.1.call-done) | data formatting | bytes 25690112 | tf_op jit(solution)/shard_map/all_gather | solution.py:160
  284.4 9.6 %convert_bitcast_fusion = bf16[8,288,4,2,112]{4,1,2,0,3:T(8,128)(2,1)} fusion(bf16[2,896,8,4,112]{1,4,3,2,0:T(8,128)(2,1)} %bitcast.141, bf16[32,896]{1,0:T(8,128)(2,1)S(1)} %slice.111, bf16[256,896]{1,0:T(8,128)(2,1)S(1)} %copy-done.3), kind=kOutput, calls=%fused_computation.6 | convolution fusion | flops 3702472704 | bytes 17489920 | tf_op jit(solution)/shard_map/tk,ckgin->gticn/dot_general | solution.py:164
  294.0 9.4 %copy.62 = bf16[8,288,4,2,112]{4,3,2,1,0:T(2,128)(2,1)} copy(bf16[8,288,4,2,112]{4,1,2,0,3:T(8,128)(2,1)} %convert_bitcast_fusion) | data formatting | bytes 8257536 | tf_op jit(solution)/shard_map/convert_element_type | solution.py:169
  303.4 15.5 %reshape.399 = bf16[8,288,896]{2,1,0:T(8,128)(2,1)} reshape(bf16[8,288,4,2,112]{4,3,2,1,0:T(2,128)(2,1)} %copy.62) | data formatting | bytes 8257536 | tf_op jit(solution)/shard_map/reshape | solution.py:170
  323.3 5.8 %collective-permute-done.11 = bf16[32,4,896]{2,0,1:T(8,128)(2,1)S(1)} collective-permute-done((bf16[32,4,896]{2,0,1:T(8,128)(2,1)S(1)}, bf16[32,4,896]{2,0,1:T(8,128)(2,1)S(1)}, u32[]{:S(2)}, u32[]{:S(2)}) %collective-permute-start.11) | collective-permute-done | bytes 229408 | tf_op jit(solution)/shard_map/ppermute | solution.py:43
  329.2 4.0 collective-permute-start.12
  333.3 5.0 %collective-permute-done.12 = bf16[32,2,896]{2,0,1:T(8,128)(2,1)S(1)} collective-permute-done((bf16[32,2,896]{2,0,1:T(8,128)(2,1)S(1)}, bf16[32,2,896]{2,0,1:T(8,128)(2,1)S(1)}, u32[]{:S(2)}, u32[]{:S(2)}) %collective-permute-start.12) | collective-permute-done | bytes 114720 | tf_op jit(solution)/shard_map/ppermute | solution.py:43
  338.3 4.3 %collective-permute-start.13 = (bf16[32,1,896]{2,0,1:T(8,128)(2,1)S(1)}, bf16[32,1,896]{2,0,1:T(8,128)(2,1)S(1)}, u32[]{:S(2)}, u32[]{:S(2)}) collective-permute-start(bf16[32,1,896]{2,0,1:T(8,128)(2,1)S(1)} %constant_dynamic-slice_fusion), channel_id=1, source_target_pairs={{0,4},{1,5},{2,6},{3,7},{4,0},{5,1},{6,2},{7,3},{8,12},{9,13},{10,... | collective-permute-start | bytes 172040 | tf_op jit(solution)/shard_map/ppermute | solution.py:43
  342.7 5.6 %collective-permute-done.13 = bf16[32,1,896]{2,0,1:T(8,128)(2,1)S(1)} collective-permute-done((bf16[32,1,896]{2,0,1:T(8,128)(2,1)S(1)}, bf16[32,1,896]{2,0,1:T(8,128)(2,1)S(1)}, u32[]{:S(2)}, u32[]{:S(2)}) %collective-permute-start.13) | collective-permute-done | bytes 57376 | tf_op jit(solution)/shard_map/ppermute | solution.py:43
  351.6 3.9 collective-permute-done.14
  355.6 3.9 collective-permute-start.15
  362.7 6.2 %collective-permute-start.16 = (bf16[32,1001]{1,0:T(8,128)(2,1)S(1)}, bf16[32,1001]{1,0:T(8,128)(2,1)S(1)}, u32[]{:S(2)}, u32[]{:S(2)}) collective-permute-start(bf16[32,1001]{1,0:T(8,128)(2,1)S(1)} %add.150), channel_id=1, source_target_pairs={{0,4},{1,5},{2,6},{3,7},{4,0},{5,1},{6,2},{7,3},{8,12},{9,13},{10,... | collective-permute-start | bytes 192200 | tf_op jit(solution)/shard_map/ppermute | solution.py:26
  368.9 5.7 %collective-permute-done.16 = bf16[32,1001]{1,0:T(8,128)(2,1)S(1)} collective-permute-done((bf16[32,1001]{1,0:T(8,128)(2,1)S(1)}, bf16[32,1001]{1,0:T(8,128)(2,1)S(1)}, u32[]{:S(2)}, u32[]{:S(2)}) %collective-permute-start.16) | collective-permute-done | bytes 64096 | tf_op jit(solution)/shard_map/ppermute | solution.py:26
  383.9 6.9 %collective-permute-start.19 = (f32[32]{0:T(128)S(1)}, f32[32]{0:T(128)S(1)}, u32[]{:S(2)}, u32[]{:S(2)}) collective-permute-start(f32[32]{0:T(128)S(1)} %max.19), channel_id=1, source_target_pairs={{0,32},{8,40},{16,48},{24,56},{32,0},{40,8},{48,16},{56,24},{64,96... | collective-permute-start | bytes 392 | tf_op jit(solution)/shard_map/ppermute | solution.py:26
  397.7 4.8 %collective-permute-start.21 = (f32[32]{0:T(128)S(1)}, f32[32]{0:T(128)S(1)}, u32[]{:S(2)}, u32[]{:S(2)}) collective-permute-start(f32[32]{0:T(128)S(1)} %max.21), channel_id=1, source_target_pairs={{0,128},{8,136},{16,144},{24,152},{32,160},{40,168},{48,176},{56,1... | collective-permute-start | bytes 392 | tf_op jit(solution)/shard_map/ppermute | solution.py:26
  404.1 6.3 %collective-permute-start.22 = (f32[32]{0:T(128)S(1)}, f32[32]{0:T(128)S(1)}, u32[]{:S(2)}, u32[]{:S(2)}) collective-permute-start(f32[32]{0:T(128)S(1)} %max.22), channel_id=1, source_target_pairs={{0,256},{8,264},{16,272},{24,280},{32,288},{40,296},{48,304},{56,3... | collective-permute-start | bytes 392 | tf_op jit(solution)/shard_map/ppermute | solution.py:26
  (123 shorter events, 96.6 us)
Async XLA Ops:
  7.2 259.2 %all-gather.2.cloned.1.call-start = ((), (), s32[]{:S(2)}) async-start(), calls=%async_computation.2 | async-start | bytes 19267584 | tf_op jit(solution)/shard_map/all_gather | solution.py:160
  176.7 237.1 %reduce-scatter.2.cloned.1.call-start = ((), (), s32[]{:S(2)}) async-start(), calls=%async_computation.3 | async-start | bytes 4644864 | tf_op jit(solution)/shard_map/reduce_scatter | solution.py:174
  176.8 21.1 %collective-permute-start = (bf16[514,128]{1,0:T(8,128)(2,1)S(1)}, bf16[514,128]{1,0:T(8,128)(2,1)}, u32[]{:S(2)}, u32[]{:S(2)}) collective-permute-start(bf16[514,128]{1,0:T(8,128)(2,1)S(1)} %pad_maximum_fusion), channel_id=1, source_target_pairs={{0,32},{8,40},{16,48},{24,56},{32,64},{40,72},{48,80},{56,88},{64,... | collective-permute-start | bytes 394760 | tf_op jit(solution)/shard_map/ppermute | solution.py:19
  180.6 18.2 %collective-permute-start.1 = (bf16[514,128]{1,0:T(8,128)(2,1)S(1)}, bf16[514,128]{1,0:T(8,128)(2,1)}, u32[]{:S(2)}, u32[]{:S(2)}) collective-permute-start(bf16[514,128]{1,0:T(8,128)(2,1)S(1)} %pad_maximum_fusion), channel_id=1, source_target_pairs={{0,24},{8,32},{16,40},{24,48},{32,56},{40,64},{48,72},{56,80},{64,... | collective-permute-start | bytes 394760 | tf_op jit(solution)/shard_map/ppermute | solution.py:19
  182.6 17.2 %collective-permute-start.2 = (bf16[514,128]{1,0:T(8,128)(2,1)S(1)}, bf16[514,128]{1,0:T(8,128)(2,1)}, u32[]{:S(2)}, u32[]{:S(2)}) collective-permute-start(bf16[514,128]{1,0:T(8,128)(2,1)S(1)} %pad_maximum_fusion), channel_id=1, source_target_pairs={{0,16},{8,24},{16,32},{24,40},{32,48},{40,56},{48,64},{56,72},{64,... | collective-permute-start | bytes 394760 | tf_op jit(solution)/shard_map/ppermute | solution.py:19
  186.0 14.7 %collective-permute-start.3 = (bf16[514,128]{1,0:T(8,128)(2,1)S(1)}, bf16[514,128]{1,0:T(8,128)(2,1)}, u32[]{:S(2)}, u32[]{:S(2)}) collective-permute-start(bf16[514,128]{1,0:T(8,128)(2,1)S(1)} %pad_maximum_fusion), channel_id=1, source_target_pairs={{0,8},{8,16},{16,24},{24,32},{32,40},{40,48},{48,56},{56,64},{64,7... | collective-permute-start | bytes 394760 | tf_op jit(solution)/shard_map/ppermute | solution.py:19
  190.6 5.1 %collective-permute-start.4 = (s32[1]{0:T(128)}, s32[1]{0:T(128)}, u32[]{:S(2)}, u32[]{:S(2)}) collective-permute-start(s32[1]{0:T(128)} %slice.109), channel_id=1, source_target_pairs={{8,0},{16,8},{24,16},{32,24},{40,32},{48,40},{56,48},{64,56},{72,6... | collective-permute-start | bytes 20 | tf_op jit(solution)/shard_map/ppermute | solution.py:19
  220.4 3.9 collective-permute-start.5
  224.4 7.3 %collective-permute-start.6 = (bf16[32,1792]{1,0:T(8,128)(2,1)S(1)}, bf16[32,1792]{1,0:T(8,128)(2,1)S(1)}, u32[]{:S(2)}, u32[]{:S(2)}) collective-permute-start(bf16[32,1792]{1,0:T(8,128)(2,1)S(1)} %add.129), channel_id=1, source_target_pairs={{0,16},{8,24},{16,0},{24,8},{32,48},{40,56},{48,32},{56,40},{64,80... | collective-permute-start | bytes 344072 | tf_op jit(solution)/shard_map/ppermute | solution.py:26
  231.8 8.2 %collective-permute-start.7 = (bf16[32,1792]{1,0:T(8,128)(2,1)S(1)}, bf16[32,1792]{1,0:T(8,128)(2,1)S(1)}, u32[]{:S(2)}, u32[]{:S(2)}) collective-permute-start(bf16[32,1792]{1,0:T(8,128)(2,1)S(1)} %add.130), channel_id=1, source_target_pairs={{0,32},{8,40},{16,48},{24,56},{32,0},{40,8},{48,16},{56,24},{64,96... | collective-permute-start | bytes 344072 | tf_op jit(solution)/shard_map/ppermute | solution.py:26
  240.0 7.0 %collective-permute-start.8 = (bf16[32,1792]{1,0:T(8,128)(2,1)S(1)}, bf16[32,1792]{1,0:T(8,128)(2,1)S(1)}, u32[]{:S(2)}, u32[]{:S(2)}) collective-permute-start(bf16[32,1792]{1,0:T(8,128)(2,1)S(1)} %add.131), channel_id=1, source_target_pairs={{0,64},{8,72},{16,80},{24,88},{32,96},{40,104},{48,112},{56,120},{... | collective-permute-start | bytes 344072 | tf_op jit(solution)/shard_map/ppermute | solution.py:26
  247.0 7.6 %collective-permute-start.9 = (bf16[32,1792]{1,0:T(8,128)(2,1)S(1)}, bf16[32,1792]{1,0:T(8,128)(2,1)S(1)}, u32[]{:S(2)}, u32[]{:S(2)}) collective-permute-start(bf16[32,1792]{1,0:T(8,128)(2,1)S(1)} %add.132), channel_id=1, source_target_pairs={{0,128},{8,136},{16,144},{24,152},{32,160},{40,168},{48,176},{56,1... | collective-permute-start | bytes 344072 | tf_op jit(solution)/shard_map/ppermute | solution.py:26
  254.6 10.7 %collective-permute-start.10 = (bf16[32,1792]{1,0:T(8,128)(2,1)S(1)}, bf16[32,1792]{1,0:T(8,128)(2,1)S(1)}, u32[]{:S(2)}, u32[]{:S(2)}) collective-permute-start(bf16[32,1792]{1,0:T(8,128)(2,1)S(1)} %add.133), channel_id=1, source_target_pairs={{0,256},{8,264},{16,272},{24,280},{32,288},{40,296},{48,304},{56,3... | collective-permute-start | bytes 344072 | tf_op jit(solution)/shard_map/ppermute | solution.py:26
  320.0 9.1 %collective-permute-start.11 = (bf16[32,4,896]{2,0,1:T(8,128)(2,1)S(1)}, bf16[32,4,896]{2,0,1:T(8,128)(2,1)S(1)}, u32[]{:S(2)}, u32[]{:S(2)}) collective-permute-start(bf16[32,4,896]{2,0,1:T(8,128)(2,1)S(1)} %dynamic-slice_bitcast_fusion), channel_id=1, source_target_pairs={{0,1},{1,0},{2,3},{3,2},{4,5},{5,4},{6,7},{7,6},{8,9},{9,8},{10,11... | collective-permute-start | bytes 688136 | tf_op jit(solution)/shard_map/ppermute | solution.py:43
  329.2 9.1 %collective-permute-start.12 = (bf16[32,2,896]{2,0,1:T(8,128)(2,1)S(1)}, bf16[32,2,896]{2,0,1:T(8,128)(2,1)S(1)}, u32[]{:S(2)}, u32[]{:S(2)}) collective-permute-start(bf16[32,2,896]{2,0,1:T(8,128)(2,1)S(1)} %dynamic-slice_bitcast_fusion.1), channel_id=1, source_target_pairs={{0,2},{1,3},{2,0},{3,1},{4,6},{5,7},{6,4},{7,5},{8,10},{9,11},{10,... | collective-permute-start | bytes 344072 | tf_op jit(solution)/shard_map/ppermute | solution.py:43
  338.3 10.0 %collective-permute-start.13 = (bf16[32,1,896]{2,0,1:T(8,128)(2,1)S(1)}, bf16[32,1,896]{2,0,1:T(8,128)(2,1)S(1)}, u32[]{:S(2)}, u32[]{:S(2)}) collective-permute-start(bf16[32,1,896]{2,0,1:T(8,128)(2,1)S(1)} %constant_dynamic-slice_fusion), channel_id=1, source_target_pairs={{0,4},{1,5},{2,6},{3,7},{4,0},{5,1},{6,2},{7,3},{8,12},{9,13},{10,... | collective-permute-start | bytes 172040 | tf_op jit(solution)/shard_map/ppermute | solution.py:43
  349.4 6.2 %collective-permute-start.14 = (bf16[32,1001]{1,0:T(8,128)(2,1)S(1)}, bf16[32,1001]{1,0:T(8,128)(2,1)S(1)}, u32[]{:S(2)}, u32[]{:S(2)}) collective-permute-start(bf16[32,1001]{1,0:T(8,128)(2,1)S(1)} %pad_maximum_fusion.2), channel_id=1, source_target_pairs={{0,1},{1,0},{2,3},{3,2},{4,5},{5,4},{6,7},{7,6},{8,9},{9,8},{10,11... | collective-permute-start | bytes 192200 | tf_op jit(solution)/shard_map/ppermute | solution.py:26
  355.6 7.1 %collective-permute-start.15 = (bf16[32,1001]{1,0:T(8,128)(2,1)S(1)}, bf16[32,1001]{1,0:T(8,128)(2,1)S(1)}, u32[]{:S(2)}, u32[]{:S(2)}) collective-permute-start(bf16[32,1001]{1,0:T(8,128)(2,1)S(1)} %fusion.63), channel_id=1, source_target_pairs={{0,2},{1,3},{2,0},{3,1},{4,6},{5,7},{6,4},{7,5},{8,10},{9,11},{10,... | collective-permute-start | bytes 192200 | tf_op jit(solution)/shard_map/ppermute | solution.py:26
  362.7 11.9 %collective-permute-start.16 = (bf16[32,1001]{1,0:T(8,128)(2,1)S(1)}, bf16[32,1001]{1,0:T(8,128)(2,1)S(1)}, u32[]{:S(2)}, u32[]{:S(2)}) collective-permute-start(bf16[32,1001]{1,0:T(8,128)(2,1)S(1)} %add.150), channel_id=1, source_target_pairs={{0,4},{1,5},{2,6},{3,7},{4,0},{5,1},{6,2},{7,3},{8,12},{9,13},{10,... | collective-permute-start | bytes 192200 | tf_op jit(solution)/shard_map/ppermute | solution.py:26
  378.5 5.4 %collective-permute-start.18 = (f32[32]{0:T(128)S(1)}, f32[32]{0:T(128)S(1)}, u32[]{:S(2)}, u32[]{:S(2)}) collective-permute-start(f32[32]{0:T(128)S(1)} %max.18), channel_id=1, source_target_pairs={{0,16},{8,24},{16,0},{24,8},{32,48},{40,56},{48,32},{56,40},{64,80... | collective-permute-start | bytes 392 | tf_op jit(solution)/shard_map/ppermute | solution.py:26
  383.9 8.4 %collective-permute-start.19 = (f32[32]{0:T(128)S(1)}, f32[32]{0:T(128)S(1)}, u32[]{:S(2)}, u32[]{:S(2)}) collective-permute-start(f32[32]{0:T(128)S(1)} %max.19), channel_id=1, source_target_pairs={{0,32},{8,40},{16,48},{24,56},{32,0},{40,8},{48,16},{56,24},{64,96... | collective-permute-start | bytes 392 | tf_op jit(solution)/shard_map/ppermute | solution.py:26
  392.3 5.4 %collective-permute-start.20 = (f32[32]{0:T(128)S(1)}, f32[32]{0:T(128)S(1)}, u32[]{:S(2)}, u32[]{:S(2)}) collective-permute-start(f32[32]{0:T(128)S(1)} %max.20), channel_id=1, source_target_pairs={{0,64},{8,72},{16,80},{24,88},{32,96},{40,104},{48,112},{56,120},{... | collective-permute-start | bytes 392 | tf_op jit(solution)/shard_map/ppermute | solution.py:26
  397.7 6.3 %collective-permute-start.21 = (f32[32]{0:T(128)S(1)}, f32[32]{0:T(128)S(1)}, u32[]{:S(2)}, u32[]{:S(2)}) collective-permute-start(f32[32]{0:T(128)S(1)} %max.21), channel_id=1, source_target_pairs={{0,128},{8,136},{16,144},{24,152},{32,160},{40,168},{48,176},{56,1... | collective-permute-start | bytes 392 | tf_op jit(solution)/shard_map/ppermute | solution.py:26
  404.1 9.3 %collective-permute-start.22 = (f32[32]{0:T(128)S(1)}, f32[32]{0:T(128)S(1)}, u32[]{:S(2)}, u32[]{:S(2)}) collective-permute-start(f32[32]{0:T(128)S(1)} %max.22), channel_id=1, source_target_pairs={{0,256},{8,264},{16,272},{24,280},{32,288},{40,296},{48,304},{56,3... | collective-permute-start | bytes 392 | tf_op jit(solution)/shard_map/ppermute | solution.py:26
  (7 other events, 442.1 us)
Sparse Core Ops, SparseCore 0:
  176.9 27.6 all-gather.1
  348.5 55.3 reduce-scatter.1
